TPU v7x, 32 devices: a whole 2x2x4 slice. The times are simulated.
32 devices in a mesh: dp: 2 (over y), expert: 16 (over z, x, core).
Axes of the slice: x: 2, y: 2, z: 4, core: 2. Of those that a mesh axis runs over, the one named last changes fastest.
Arguments:
- tokens: bfloat16 [4096, 1024], P(('dp', 'expert')), may hold values from -6 to 6
- masked: int32 [4096], P(('dp', 'expert')), may hold values 0 or 1
- importance: float32 [4096], P(('dp', 'expert')), may hold values from 1 to 10
- routes: int32 [4096, 8], P(('dp', 'expert')), may hold values from 0 to 15, all different within a row; in each aligned block of 128 rows (0 to 127, 128 to 255, ...) at most 96 rows name the same one
- gates: float32 [4096, 8], P(('dp', 'expert')), may hold values from 0.05 to 0.3
- cotangent: bfloat16 [4096, 1024], P(('dp', 'expert')), may hold values from -6 to 6
- w_gate: bfloat16 [16, 512, 1024], P('expert'), may hold values from -0.1875 to 0.1875
- w_up: bfloat16 [16, 512, 1024], P('expert'), may hold values from -0.1875 to 0.1875
- w_down: bfloat16 [16, 512, 1024], P('expert'), may hold values from -0.25 to 0.25
Outputs:
- mixed: bfloat16 [4096, 1024], P(('dp', 'expert'))
- weight_grads: float32 [16, 512, 3, 1024], P('expert', 'dp')
Inputs may be any that keep to these rules, and one draw needn't show every extreme that they name: `routes`: among the 128 rows of one device (aligned blocks of rows), no expert is named by more than 96 rows, a bound that some block reaches; a row names 8 different experts.
All inputs are finite; a program needn't handle non-finite values. No bound on the sum of `masked` on one device may be relied on, other than what follows from the above.
Results may differ from a plain program's by a relative error of at most 0.0057.
Values may be sent and summed in bfloat16 or wider, within the bound.
No kernel may reach another device: no remote copies, remote signals or barrier semaphores. Data moves between devices by JAX's collectives and lax.ppermute only.
A program may use at most 64 MiB of HBM per device.

v0:
```python
import jax
import jax.numpy as jnp
from jax import lax
from jax.sharding import PartitionSpec as P

GATHER_ROWS = 2048
RETURN = "scatter"


def contract_rows(left, right):
    return lax.dot_general(
        left, right, (((0,), (0,)), ((), ())), preferred_element_type=jnp.float32
    )


def contract_cols(left, right):
    return lax.dot_general(
        left, right, (((1,), (1,)), ((), ())), preferred_element_type=jnp.float32
    )


def expert_math(rows_x, rows_q, wgate, wup, wdown):
    gate_pre = contract_cols(rows_x, wgate)
    up_pre = contract_cols(rows_x, wup)
    sig = jax.nn.sigmoid(gate_pre)
    act = gate_pre * sig
    hidden = (act * up_pre).astype(jnp.bfloat16)
    expert_out = jnp.dot(hidden, wdown, preferred_element_type=jnp.float32).astype(jnp.bfloat16)
    back = contract_cols(rows_q, wdown)
    d_gate = (back * up_pre * sig * (1.0 + gate_pre * (1.0 - sig))).astype(jnp.bfloat16)
    d_up = (back * act).astype(jnp.bfloat16)
    grad_gate = contract_rows(d_gate, rows_x)
    grad_up = contract_rows(d_up, rows_x)
    grad_down = contract_rows(hidden, rows_q)
    return (expert_out, jnp.stack([grad_gate, grad_up, grad_down], axis=1))


def reduce_grads(grads, width):
    share = grads.shape[0] // lax.axis_size("dp")
    summed = lax.psum_scatter(grads, "dp", scatter_dimension=0, tiled=True)
    return summed.reshape(1, share, 3, width)


def source_slots(routes, experts):
    flat = routes.reshape(-1)
    onehot = (flat[:, None] == jnp.arange(experts, dtype=jnp.int32)[None, :]).astype(jnp.int32)
    before = jnp.cumsum(onehot, axis=0) - onehot
    return (flat, jnp.sum(before * onehot, axis=1))


def local_a2a(tokens, masked, importance, routes, gates, cotangent, w_gate, w_up, w_down):
    tok_rows = tokens.shape[0]
    width = tokens.shape[1]
    topk = routes.shape[1]
    experts = lax.axis_size("expert")
    capacity = min(tok_rows, 3 * tok_rows * topk // (2 * experts))
    flat, slots = source_slots(routes, experts)
    target = flat * capacity + slots
    owner = jnp.arange(tok_rows * topk, dtype=jnp.int32) // topk
    coef = importance * masked.astype(jnp.float32)
    factor = (coef[:, None] * gates).reshape(-1)
    sent_x = jnp.zeros((experts * capacity, width), jnp.bfloat16).at[target].set(tokens[owner])
    scaled = (factor[:, None] * cotangent[owner].astype(jnp.float32)).astype(jnp.bfloat16)
    sent_q = jnp.zeros((experts * capacity, width), jnp.bfloat16).at[target].set(scaled)
    layout = (experts, capacity, width)
    recv_x = lax.all_to_all(sent_x.reshape(layout), "expert", 0, 0, tiled=True)
    recv_q = lax.all_to_all(sent_q.reshape(layout), "expert", 0, 0, tiled=True)
    expert_out, grads = expert_math(
        recv_x.reshape(-1, width), recv_q.reshape(-1, width), w_gate[0], w_up[0], w_down[0]
    )
    returned = lax.all_to_all(expert_out.reshape(layout), "expert", 0, 0, tiled=True)
    picked = returned.reshape(-1, width)[target].astype(jnp.float32)
    summed = jnp.sum(picked.reshape(tok_rows, topk, width) * gates[:, :, None], axis=1)
    return (summed.astype(jnp.bfloat16), reduce_grads(grads, width))


def local_gather(tokens, masked, importance, routes, gates, cotangent, w_gate, w_up, w_down):
    tok_rows = tokens.shape[0]
    width = tokens.shape[1]
    topk = routes.shape[1]
    experts = lax.axis_size("expert")
    capacity = min(tok_rows, 3 * tok_rows * topk // (2 * experts))
    me = lax.axis_index("expert")
    coef = importance * masked.astype(jnp.float32)
    factor = coef[:, None] * gates
    meta = jnp.concatenate([routes.astype(jnp.float32), factor, gates], axis=1)
    all_x = lax.all_gather(tokens, "expert", axis=0, tiled=True)
    all_meta = lax.all_gather(meta, "expert", axis=0, tiled=True)
    all_c = lax.all_gather(cotangent, "expert", axis=0, tiled=True)
    all_routes = all_meta[:, :topk].astype(jnp.int32)
    hit = all_routes == me
    zero = jnp.zeros((), jnp.float32)
    fac = jnp.sum(jnp.where(hit, all_meta[:, topk : 2 * topk], zero), axis=1)
    gte = jnp.sum(jnp.where(hit, all_meta[:, 2 * topk :], zero), axis=1)
    routed = jnp.any(hit, axis=1).reshape(experts, tok_rows)
    ahead = (
        lax.broadcasted_iota(jnp.int32, (tok_rows, tok_rows), 0)
        < lax.broadcasted_iota(jnp.int32, (tok_rows, tok_rows), 1)
    ).astype(jnp.bfloat16)
    rank = jnp.dot(routed.astype(jnp.bfloat16), ahead, preferred_element_type=jnp.float32).astype(
        jnp.int32
    )
    slot_ids = lax.broadcasted_iota(jnp.int32, (experts, capacity, tok_rows), 1)
    pick = (routed[:, None, :] & (rank[:, None, :] == slot_ids)).astype(jnp.bfloat16)

    def select(values):
        rows = jnp.einsum(
            "sjt,std->sjd",
            pick,
            values.reshape(experts, tok_rows, width),
            preferred_element_type=jnp.float32,
        )
        return rows.astype(jnp.bfloat16).reshape(experts * capacity, width)

    rows_x = select(all_x)
    all_q = (fac[:, None] * all_c.astype(jnp.float32)).astype(jnp.bfloat16)
    rows_q = select(all_q)
    expert_out, grads = expert_math(rows_x, rows_q, w_gate[0], w_up[0], w_down[0])
    if RETURN == "scatter":
        dense = jnp.einsum(
            "sjt,sjd->std",
            pick,
            expert_out.reshape(experts, capacity, width),
            preferred_element_type=jnp.float32,
        ).reshape(experts * tok_rows, width)
        contrib = gte[:, None] * dense
        summed = lax.psum_scatter(contrib, "expert", scatter_dimension=0, tiled=True)
    else:
        returned = lax.all_to_all(
            expert_out.reshape(experts, capacity, width), "expert", 0, 0, tiled=True
        )
        flat, slots = source_slots(routes, experts)
        target = flat * capacity + slots
        choose = (
            target[:, None]
            == lax.broadcasted_iota(jnp.int32, (tok_rows * topk, experts * capacity), 1)
        ).astype(jnp.bfloat16)
        picked = jnp.dot(choose, returned.reshape(-1, width), preferred_element_type=jnp.float32)
        summed = jnp.sum(picked.reshape(tok_rows, topk, width) * gates[:, :, None], axis=1)
    return (summed.astype(jnp.bfloat16), reduce_grads(grads, width))


def local(*args):
    tokens = args[0]
    if lax.axis_size("expert") * tokens.shape[0] <= GATHER_ROWS:
        return local_gather(*args)
    return local_a2a(*args)


def solution(mesh):
    in_specs = (
        P(("dp", "expert"), None),
        P(("dp", "expert")),
        P(("dp", "expert")),
        P(("dp", "expert"), None),
        P(("dp", "expert"), None),
        P(("dp", "expert"), None),
        P("expert", None, None),
        P("expert", None, None),
        P("expert", None, None),
    )
    out_specs = (P(("dp", "expert"), None), P("expert", "dp", None, None))
    return jax.shard_map(local, mesh=mesh, in_specs=in_specs, out_specs=out_specs, check_vma=False)
```

profile of v0, /device:TPU:0, one launch (start us, length us, event | category | flops | bytes accessed | tf_op | source)
XLA Modules:
  0.0 308.5 jit_solution(12384886933002429471)
XLA Ops:
  7.2 0.0 copy-start
  7.2 0.0 all-gather.3.cloned.1.call-start
  7.2 0.7 all-gather.3.cloned.1.call-update
  7.9 0.0 all-gather.5.cloned.1.call-start
  8.0 0.7 all-gather.5.cloned.1.call-update
  8.7 0.0 reduce-scatter.3.cloned.1.call-start
  8.7 0.7 convert_element_type.42
  9.4 0.7 convert_multiply_fusion
  10.1 0.7 broadcast_multiply_fusion
  10.8 0.7 pad_maximum_fusion.1
  11.5 23.8 %all_gather.9 = f32[2048,24]{0,1:T(8,128)S(1)} all-gather(f32[128,24]{0,1:T(8,128)S(1)} %pad_maximum_fusion.1), channel_id=1, replica_groups=mesh['dp'=2,'expert'=16] {'expert'}, dimensions={0}, use_global_device_ids=true | all-gather | bytes 208896 | tf_op jit(solution)/shard_map/all_gather | solution.py:88
  35.3 0.1 fusion.20
  35.4 0.1 convolution_convert_fusion.3
  35.5 28.4 %all-gather.3.cloned.1.call-done = bf16[2048,1024]{1,0:T(8,128)(2,1)} async-done(((bf16[128,1024]{1,0:T(8,128)(2,1)}), bf16[2048,1024]{1,0:T(8,128)(2,1)}) %all-gather.3.cloned.1.call-update) | async-done | bytes 4194320 | tf_op jit(solution)/shard_map/all_gather | solution.py:87
  63.9 0.0 copy-start.3
  63.9 3.2 %convolution_convert_fusion.2 = bf16[16,96,1024]{2,1,0:T(8,128)(2,1)S(1)} fusion(bf16[16,128,1024]{2,1,0:T(8,128)(2,1)} %bitcast.42, s32[16,128]{1,0:T(8,128)S(1)} %convolution_convert_fusion.3, pred[16,128]{1,0:T(8,128)(4,1)S(1)} %bitcast.50), kind=kOutput, calls=%fused_computation.10 | convolution fusion | flops 404619264 | bytes 7350272 | tf_op jit(solution)/shard_map/sjt,std->sjd/dot_general | solution.py:107
  67.2 0.0 copy-start.1
  67.2 0.0 copy-done.3
  67.2 0.0 copy-start.4
  67.2 1.8 fusion.6
  69.0 0.0 copy-done.1
  69.0 0.2 copy-done.4
  69.2 0.0 copy-start.5
  69.2 3.9 %multiply_convert_fusion.3 = (bf16[1536,512]{1,0:T(8,128)(2,1)S(1)}, f32[1536,512]{1,0:T(8,128)}) fusion(f32[1536,512]{1,0:T(8,128)S(1)} %fusion.6, bf16[1536,1024]{1,0:T(8,128)(2,1)S(1)} %bitcast.44, bf16[1,512,1024]{2,1,0:T(8,128)(2,1)S(1)} %copy-done.4), kind=kOutput, calls=%fused_computation.6 | convolution fusion | flops 1615331328 | bytes 12058624 | tf_op jit(solution)/shard_map/dot_general | solution.py:17
  73.2 0.0 copy-done.5
  73.2 0.0 copy-done
  73.2 1.8 convolution_convert_fusion
  75.0 1.3 fusion.10
  76.3 3.9 %bitcast_multiply_fusion = f32[2048,1024]{1,0:T(8,128)} fusion(f32[16,128,1024]{2,1,0:T(8,128)S(1)} %fusion.10, f32[2048]{0:T(1024)S(1)} %get-tuple-element.3), kind=kLoop, calls=%fused_computation | loop fusion | flops 2097152 | bytes 16785408 | tf_op jit(solution)/shard_map/mul | solution.py:126
  80.2 0.0 reduce-scatter.3.cloned.1.call-update
  80.2 0.2 reduce-scatter.5.cloned.1.call-start
  80.4 34.7 %all-gather.5.cloned.1.call-done = bf16[2048,1024]{1,0:T(8,128)(2,1)} async-done(((bf16[128,1024]{1,0:T(8,128)(2,1)}), bf16[2048,1024]{1,0:T(8,128)(2,1)}) %all-gather.5.cloned.1.call-update) | async-done | bytes 4194320 | tf_op jit(solution)/shard_map/all_gather | solution.py:89
  115.1 2.9 multiply_convert_fusion
  118.1 1.0 convolution_convert_fusion.1
  119.1 1.8 fusion.1
  120.9 0.0 copy-start.2
  120.9 0.0 copy-start.6
  120.9 1.8 convolution_bitcast_fusion
  122.8 0.0 copy-done.2
  122.8 1.3 copy-done.6
  124.1 0.0 copy-start.7
  124.1 1.9 convolution_bitcast_fusion.1
  126.0 0.3 copy-done.7
  126.4 2.5 convolution_bitcast_fusion.2
  128.9 3.4 %pad_maximum_fusion = f32[512,3,1024]{2,0,1:T(8,128)} fusion(f32[512,1,1024]{2,0,1:T(8,128)S(1)} %convolution_bitcast_fusion, f32[512,1,1024]{2,0,1:T(8,128)S(1)} %convolution_bitcast_fusion.1, f32[512,1,1024]{2,0,1:T(8,128)S(1)} %convolution_bitcast_fusion.2), kind=kLoop, calls=%fused_computation.2 | loop fusion | flops 3145728 | bytes 12582912 | tf_op jit(solution)/shard_map/stack | solution.py:35
  132.2 0.0 reduce-scatter.5.cloned.1.call-update
  132.2 90.1 %reduce-scatter.3.cloned.1.call-done = f32[128,1024]{1,0:T(8,128)} async-done(((f32[2048,1024]{1,0:T(8,128)}), f32[128,1024]{1,0:T(8,128)}) %reduce-scatter.3.cloned.1.call-update) | async-done | bytes 524304 | tf_op jit(solution)/shard_map/reduce_scatter | solution.py:127
  222.4 1.8 convert_element_type.49
  224.2 77.8 %reduce-scatter.5.cloned.1.call-done = f32[256,3,1024]{2,0,1:T(8,128)} async-done(((f32[512,3,1024]{2,0,1:T(8,128)}), f32[256,3,1024]{2,0,1:T(8,128)}) %reduce-scatter.5.cloned.1.call-update) | async-done | bytes 3145744 | tf_op jit(solution)/shard_map/reduce_scatter | solution.py:40
  (1 shorter events, 0.0 us)
Async XLA Ops:
  7.2 66.0 %copy-start = (bf16[1,512,1024]{2,1,0:T(8,128)(2,1)S(1)}, bf16[1,512,1024]{2,1,0:T(8,128)(2,1)}, u32[]{:S(2)}) copy-start(bf16[1,512,1024]{2,1,0:T(8,128)(2,1)} %param.17) | copy-start | bytes 3145732
  7.2 56.7 %all-gather.3.cloned.1.call-start = ((), (), s32[]{:S(2)}) async-start(), calls=%async_computation.2 | async-start | bytes 4456448 | tf_op jit(solution)/shard_map/all_gather | solution.py:87
  7.9 107.2 %all-gather.5.cloned.1.call-start = ((), (), s32[]{:S(2)}) async-start(), calls=%async_computation.4 | async-start | bytes 4456448 | tf_op jit(solution)/shard_map/all_gather | solution.py:89
  8.7 213.7 %reduce-scatter.3.cloned.1.call-start = ((), (), s32[]{:S(2)}) async-start(), calls=%async_computation.3 | async-start | bytes 8912896 | tf_op jit(solution)/shard_map/reduce_scatter | solution.py:127
  63.9 3.3 %copy-start.3 = (bf16[1,512,1024]{2,1,0:T(8,128)(2,1)S(1)}, bf16[1,512,1024]{2,1,0:T(8,128)(2,1)}, u32[]{:S(2)}) copy-start(bf16[1,512,1024]{2,1,0:T(8,128)(2,1)} %param.15) | copy-start | bytes 3145732
  67.2 1.9 copy-start.1
  67.2 2.0 copy-start.4
  69.2 3.9 %copy-start.5 = (f32[1536,512]{1,0:T(8,128)}, f32[1536,512]{1,0:T(8,128)S(1)}, u32[]{:S(2)}) copy-start(f32[1536,512]{1,0:T(8,128)S(1)} %fusion.6) | copy-start | bytes 9437188
  80.2 221.8 %reduce-scatter.5.cloned.1.call-start = ((), (), s32[]{:S(2)}) async-start(), calls=%async_computation.5 | async-start | bytes 9437184 | tf_op jit(solution)/shard_map/reduce_scatter | solution.py:40
  120.9 1.9 copy-start.2
  120.9 3.2 %copy-start.6 = (f32[1536,512]{1,0:T(8,128)S(1)}, f32[1536,512]{1,0:T(8,128)}, u32[]{:S(2)}) copy-start(f32[1536,512]{1,0:T(8,128)} %copy-done.5) | copy-start | bytes 9437188
  124.1 2.3 copy-start.7
Sparse Core Ops, SparseCore 0:
  10.2 53.6 all-gather.2
  66.1 49.0 all-gather.4
  119.2 103.1 reduce-scatter.2
  225.1 76.7 reduce-scatter.4
where the time goes:
time: 309 us; the launch traced here: 308 us
  waiting for transfers between devices  232 us (75%)
  blocking collectives  23.8 us (8%)
  matrix products  21.4 us (7%)
  other arithmetic  14.7 us (5%)
  between operations  13.9 us (4%)
    reduce_scatter x1, waiting for transfers between devices, local_gather(): lax.psum_scatter(contrib, 'expert', scatter_dimension=0, tiled=True)  90.1 us
    reduce_scatter x1, waiting for transfers between devices, reduce_grads(): summed = lax.psum_scatter(grads, 'dp', scatter_dimension=0, tiled=True)  77.8 us
    all_gather x1, waiting for transfers between devices, local_gather(): all_c = lax.all_gather(cotangent, 'expert', axis=0, tiled=True)  34.7 us
    all_gather x1, waiting for transfers between devices, local_gather(): all_x = lax.all_gather(tokens, 'expert', axis=0, tiled=True)  28.4 us
    all_gather x1, blocking collectives, local_gather(): all_meta = lax.all_gather(meta, 'expert', axis=0, tiled=True)  23.8 us
    dot_general x3, matrix products, contract_cols(): lax.dot_general(left, right, (((1,), (1,)), ((), ())), preferred_element_...  7.63 us
    dot_general x3, matrix products, contract_rows(): lax.dot_general(left, right, (((0,), (0,)), ((), ())), preferred_element_...  6.24 us
  transfers between devices with their start and end apart: 4, of which 4 were waited for; matrix products, arithmetic and copies ran while one was open for 12% of the time, Pallas kernels for 0%

commit v1 on v0

--- a/solution.py
+++ b/solution.py
@@ -5,6 +5,14 @@
 
 GATHER_ROWS = 2048
 RETURN = "scatter"
+
+
+def process_leaf_here(raw, mine_x):
+    return jnp.split(
+        lax.all_gather(jnp.concatenate([raw, mine_x], 1), "expert", tiled=True, axis=0),
+        [raw.shape[1]],
+        1,
+    )
 
 
 def contract_rows(left, right):
@@ -85,8 +93,7 @@
     factor = coef[:, None] * gates
     meta = jnp.concatenate([routes.astype(jnp.float32), factor, gates], axis=1)
     all_x = lax.all_gather(tokens, "expert", axis=0, tiled=True)
-    all_meta = lax.all_gather(meta, "expert", axis=0, tiled=True)
-    all_c = lax.all_gather(cotangent, "expert", axis=0, tiled=True)
+    all_meta, all_c = process_leaf_here(meta, cotangent)
     all_routes = all_meta[:, :topk].astype(jnp.int32)
     hit = all_routes == me
     zero = jnp.zeros((), jnp.float32)

time: 309 us -> 356 us (1.15)
  waiting for transfers between devices: 232 us -> 295 us
  blocking collectives: 23.8 us -> 0 us
  local copies, waits for them, and re-layouts: 1.87 us -> 6.05 us
    all_gather x1, waiting for transfers between devices: 34.7 us -> 83.5 us  [process_leaf_here(): lax.all_gather(jnp.concatenate([raw, mine_x], 1), 'expert', tiled=True, a...]
    all_gather x1 -> x0, blocking collectives: 23.8 us -> none  [local_gather(): all_meta = lax.all_gather(meta, 'expert', axis=0, tiled=True)]
    all_gather x1, waiting for transfers between devices: 28.4 us -> 46.9 us  [local_gather(): all_x = lax.all_gather(tokens, 'expert', axis=0, tiled=True)]
    mul x1 -> x0, other arithmetic: 3.85 us -> none  [local_gather(): contrib = gte[:, None] * dense]
    reduce_scatter x1, waiting for transfers between devices: 90.1 us -> 86.3 us  [local_gather(): lax.psum_scatter(contrib, 'expert', scatter_dimension=0, tiled=True)]
  transfers between devices with their start and end apart: 4 -> 4, of which waited for: 4 -> 4; matrix products, arithmetic and copies ran while one was open for 12% -> 6% of each run, Pallas kernels for 0% -> 0%
where the time goes in v1:
time: 356 us
  waiting for transfers between devices  295 us (83%)
  matrix products  23.5 us (7%)
  other arithmetic  16.7 us (5%)
  between operations  13.9 us (4%)
  local copies, waits for them, and re-layouts  6.05 us (2%)
    reduce_scatter x1, waiting for transfers between devices, local_gather(): lax.psum_scatter(contrib, 'expert', scatter_dimension=0, tiled=True)  86.3 us
    all_gather x1, waiting for transfers between devices, process_leaf_here(): lax.all_gather(jnp.concatenate([raw, mine_x], 1), 'expert', tiled=True, a...  83.5 us
    reduce_scatter x1, waiting for transfers between devices, reduce_grads(): summed = lax.psum_scatter(grads, 'dp', scatter_dimension=0, tiled=True)  77.8 us
    all_gather x1, waiting for transfers between devices, local_gather(): all_x = lax.all_gather(tokens, 'expert', axis=0, tiled=True)  46.9 us
    dot_general x3, matrix products, contract_cols(): lax.dot_general(left, right, (((1,), (1,)), ((), ())), preferred_element_...  7.63 us
  transfers between devices with their start and end apart: 4, of which 4 were waited for; matrix products, arithmetic and copies ran while one was open for 6% of the time, Pallas kernels for 0%

profile of v1, /device:TPU:0, one launch (start us, length us, event | category | flops | bytes accessed | tf_op | source)
XLA Modules:
  0.0 355.8 jit_solution(6452393381387110321)
XLA Ops:
  7.2 0.0 copy-start
  7.2 0.0 all-gather.3.cloned.1.call-start
  7.2 0.9 copy.17
  8.1 0.7 convert_multiply_fusion
  8.8 0.7 broadcast_multiply_fusion
  9.5 0.7 convert_element_type.42
  10.1 0.1 copy.15
  10.3 0.1 copy.16
  10.4 2.0 concatenate.3
  12.4 0.0 all-gather.3.cloned.1.call-update
  12.4 0.0 all-gather.5.cloned.1.call-start
  12.5 0.7 all-gather.5.cloned.1.call-update
  13.2 0.0 reduce-scatter.3.cloned.1.call-start
  13.2 83.5 %all-gather.3.cloned.1.call-done = f32[2048,1048]{1,0:T(8,128)} async-done(((f32[128,1048]{1,0:T(8,128)}), f32[2048,1048]{1,0:T(8,128)}) %all-gather.3.cloned.1.call-update) | async-done | bytes 8585232 | tf_op jit(solution)/shard_map/all_gather | solution.py:12
  96.7 3.5 fusion.2
  100.2 0.3 reduce_or.9
  100.6 0.1 convolution_convert_fusion.3
  100.7 46.9 %all-gather.5.cloned.1.call-done = bf16[2048,1024]{1,0:T(8,128)(2,1)} async-done(((bf16[128,1024]{1,0:T(8,128)(2,1)}), bf16[2048,1024]{1,0:T(8,128)(2,1)}) %all-gather.5.cloned.1.call-update) | async-done | bytes 4194320 | tf_op jit(solution)/shard_map/all_gather | solution.py:95
  147.6 0.0 copy-start.3
  147.6 3.2 convolution_convert_fusion.2
  150.9 0.0 copy-start.1
  150.9 0.0 copy-done.3
  150.9 0.0 copy-start.4
  150.9 1.8 fusion.10
  152.7 0.0 copy-done.1
  152.8 0.2 copy-done.4
  152.9 0.0 copy-start.5
  152.9 3.9 %multiply_convert_fusion.2 = (bf16[1536,512]{1,0:T(8,128)(2,1)S(1)}, f32[1536,512]{1,0:T(8,128)}) fusion(f32[1536,512]{1,0:T(8,128)S(1)} %fusion.10, bf16[1536,1024]{1,0:T(8,128)(2,1)S(1)} %bitcast.46, bf16[1,512,1024]{2,1,0:T(8,128)(2,1)S(1)} %copy-done.4), kind=kOutput, calls=%fused_computation.7 | convolution fusion | flops 1615331328 | bytes 12058624 | tf_op jit(solution)/shard_map/dot_general | solution.py:25
  156.9 0.0 copy-done.5
  156.9 0.0 copy-done
  156.9 0.0 slice-start
  156.9 0.0 slice-start.1
  156.9 1.8 convolution_convert_fusion
  158.7 0.0 slice-start.2
  158.7 1.3 fusion.14
  160.0 0.0 slice-done
  160.1 0.3 slice-done.1
  160.3 0.4 slice-done.2
  160.8 5.6 %fusion = (bf16[2048,1024]{1,0:T(8,128)(2,1)}, f32[2048,1024]{1,0:T(8,128)}) fusion(f32[2048,1048]{1,0:T(8,128)S(1)} %bitcast.43, f32[2048]{0:T(1024)S(1)} %get-tuple-element.2, f32[16,128,1024]{2,1,0:T(8,128)S(1)} %fusion.14, f32[2048]{0:T(1024)S(1)} %get-tuple-element.3), kind=kLoop, calls=%fused_computation.1 | loop fusion | flops 6291456 | bytes 29376512 | tf_op jit(solution)/shard_map/convert_element_type | solution.py:123
  166.4 0.0 reduce-scatter.3.cloned.1.call-update
  166.4 0.2 reduce-scatter.5.cloned.1.call-start
  166.6 3.2 convolution_convert_fusion.1
  169.8 1.8 fusion.5
  171.7 0.0 copy-start.2
  171.7 0.0 copy-start.6
  171.7 1.8 convolution_bitcast_fusion
  173.5 0.4 copy-done.2
  173.9 1.3 copy-done.6
  175.2 0.0 copy-start.7
  175.2 1.9 convolution_bitcast_fusion.1
  177.1 0.3 copy-done.7
  177.5 2.5 convolution_bitcast_fusion.2
  180.0 3.4 pad_maximum_fusion
  183.3 0.0 reduce-scatter.5.cloned.1.call-update
  183.4 86.3 %reduce-scatter.3.cloned.1.call-done = f32[128,1024]{1,0:T(8,128)} async-done(((f32[2048,1024]{1,0:T(8,128)}), f32[128,1024]{1,0:T(8,128)}) %reduce-scatter.3.cloned.1.call-update) | async-done | bytes 524304 | tf_op jit(solution)/shard_map/reduce_scatter | solution.py:134
  269.7 1.8 convert_element_type.50
  271.4 77.8 %reduce-scatter.5.cloned.1.call-done = f32[256,3,1024]{2,0,1:T(8,128)} async-done(((f32[512,3,1024]{2,0,1:T(8,128)}), f32[256,3,1024]{2,0,1:T(8,128)}) %reduce-scatter.5.cloned.1.call-update) | async-done | bytes 3145744 | tf_op jit(solution)/shard_map/reduce_scatter | solution.py:48
  (1 shorter events, 0.0 us)
Async XLA Ops:
  7.2 149.7 %copy-start = (bf16[1,512,1024]{2,1,0:T(8,128)(2,1)S(1)}, bf16[1,512,1024]{2,1,0:T(8,128)(2,1)}, u32[]{:S(2)}) copy-start(bf16[1,512,1024]{2,1,0:T(8,128)(2,1)} %param.17) | copy-start | bytes 3145732
  7.2 89.5 %all-gather.3.cloned.1.call-start = ((), (), s32[]{:S(2)}) async-start(), calls=%async_computation.2 | async-start | bytes 10027008 | tf_op jit(solution)/shard_map/all_gather | solution.py:12
  12.4 135.2 %all-gather.5.cloned.1.call-start = ((), (), s32[]{:S(2)}) async-start(), calls=%async_computation.3 | async-start | bytes 4456448 | tf_op jit(solution)/shard_map/all_gather | solution.py:95
  13.2 256.5 %reduce-scatter.3.cloned.1.call-start = ((), (), s32[]{:S(2)}) async-start(), calls=%async_computation.4 | async-start | bytes 8912896 | tf_op jit(solution)/shard_map/reduce_scatter | solution.py:134
  147.6 3.3 copy-start.3
  150.9 1.9 copy-start.1
  150.9 2.0 copy-start.4
  152.9 3.9 %copy-start.5 = (f32[1536,512]{1,0:T(8,128)}, f32[1536,512]{1,0:T(8,128)S(1)}, u32[]{:S(2)}) copy-start(f32[1536,512]{1,0:T(8,128)S(1)} %fusion.10) | copy-start | bytes 9437188
  156.9 3.2 slice-start
  156.9 3.5 slice-start.1
  158.7 2.0 slice-start.2
  166.4 182.9 %reduce-scatter.5.cloned.1.call-start = ((), (), s32[]{:S(2)}) async-start(), calls=%async_computation.5 | async-start | bytes 9437184 | tf_op jit(solution)/shard_map/reduce_scatter | solution.py:48
  171.7 2.3 copy-start.2
  171.7 3.6 %copy-start.6 = (f32[1536,512]{1,0:T(8,128)S(1)}, f32[1536,512]{1,0:T(8,128)}, u32[]{:S(2)}) copy-start(f32[1536,512]{1,0:T(8,128)} %copy-done.5) | copy-start | bytes 9437188
  175.2 2.2 copy-start.7
Sparse Core Ops, SparseCore 0:
  12.5 84.1 all-gather.2
  98.9 48.7 all-gather.4
  166.5 103.0 reduce-scatter.2
  272.4 76.8 reduce-scatter.4
